TPU v7x, 32 devices: a whole 2x2x4 slice. The times are simulated.
32 devices in a mesh: seq: 16 (over z, y, core), fsdp: 2 (over x).
Axes of the slice: x: 2, y: 2, z: 4, core: 2. Of those that a mesh axis runs over, the one named last changes fastest.
Arguments:
- queries: bfloat16 [2, 8192, 1024], P('fsdp', 'seq'), may hold values from -10.5 to 10.5
- key_vectors: bfloat16 [2, 8192, 1024], P('fsdp', 'seq'), may hold values from -10.5 to 10.5
- value_vectors: bfloat16 [2, 8192, 1024], P('fsdp', 'seq'), may hold values from -6 to 6
- grad_mixed: bfloat16 [2, 8192, 2048], P('fsdp', 'seq'), may hold values from -24 to 24
- out_weight: bfloat16 [1024, 2048], P('fsdp'), may hold values from -0.1875 to 0.1875
- head_phase: int32 [8], replicated, may hold values from 0 to 3
- segments_short: int32 [7], replicated, may hold values from 1 to 2048, 8192 in all
- segments_long: int32 [1], replicated, may hold values from 1 to 8192, as said below
Outputs:
- grad_query: bfloat16 [2, 8192, 1024], P('fsdp', 'seq')
- grad_key: bfloat16 [2, 8192, 1024], P('fsdp', 'seq')
- grad_value: bfloat16 [2, 8192, 1024], P('fsdp', 'seq')
Inputs may be any that keep to these rules, and one draw needn't show every extreme that they name: `segments_long`: lengths that sum to 8192; the last of them is 8192, the others are shorter.
All inputs are finite; a program needn't handle non-finite values.
Results may differ from a plain program's by a relative error of at most 0.0095.
Values may be sent and summed in bfloat16 or wider, within the bound.
No kernel may reach another device: no remote copies, remote signals or barrier semaphores. Data moves between devices by JAX's collectives and lax.ppermute only.
A program may use at most 256 MiB of HBM per device.

v0:
```python
import functools
import math

import jax
import jax.numpy as jnp
from jax import lax
from jax.experimental import pallas as pl
from jax.experimental.pallas import tpu as pltpu
from jax.sharding import PartitionSpec as P


REACH_SHORT = 4


VERY_NEGATIVE = -1e30


def passed_along(value, axis, by):
    devices = lax.axis_size(axis)
    pairs = [(i, i + by) for i in range(devices) if 0 <= i + by < devices]
    return lax.ppermute(value, axis, pairs)


def take_rows(tensor, parity):
    layout = tensor.shape
    paired = tensor.reshape(layout[:-2] + (layout[-2] // 2, 2, layout[-1]))
    return jnp.where((parity == 0)[:, None, None], paired[..., 0, :], paired[..., 1, :])


def put_rows(tensor, parity):
    zero_fill = jnp.zeros_like(tensor)
    first_half = jnp.where((parity == 0)[:, None, None], tensor, zero_fill)
    second_half = jnp.where((parity == 1)[:, None, None], tensor, zero_fill)
    stacked = jnp.stack([first_half, second_half], axis=-2)
    return stacked.reshape(tensor.shape[:-2] + (2 * tensor.shape[-2], tensor.shape[-1]))


def take_stats(tensor, parity):
    paired = tensor.reshape(tensor.shape[:-1] + (tensor.shape[-1] // 2, 2))
    return jnp.where((parity == 0)[:, None, None], paired[..., 0], paired[..., 1])


def pick_last(tensor, parity):
    paired = tensor.reshape(tensor.shape[:-1] + (tensor.shape[-1] // 2, 2))
    cond = (parity == 0).reshape((-1,) + (1,) * (tensor.ndim - 1))
    return jnp.where(cond, paired[..., 0], paired[..., 1])


def put_last(tensor, parity):
    cond = (parity == 0).reshape((-1,) + (1,) * (tensor.ndim - 1))
    zero_fill = jnp.zeros_like(tensor)
    stacked = jnp.stack(
        [jnp.where(cond, tensor, zero_fill), jnp.where(cond, zero_fill, tensor)], axis=-1
    )
    return stacked.reshape(tensor.shape[:-1] + (2 * tensor.shape[-1],))


def order_rows(tensor, parity):
    return jnp.concatenate([take_rows(tensor, parity), take_rows(tensor, 1 - parity)], axis=-2)


def unorder_rows(tensor, parity):
    half = tensor.shape[-2] // 2
    return put_rows(tensor[..., :half, :], parity) + put_rows(tensor[..., half:, :], 1 - parity)


def order_last(tensor, parity):
    return jnp.concatenate([pick_last(tensor, parity), pick_last(tensor, 1 - parity)], axis=-1)


def unorder_last(tensor, parity):
    half = tensor.shape[-1] // 2
    return put_last(tensor[..., :half], parity) + put_last(tensor[..., half:], 1 - parity)


def segment_of(positions, lengths):
    seg_ends = jnp.cumsum(lengths)
    return jnp.sum((positions[..., None] >= seg_ends).astype(jnp.int32), axis=-1)


def row_positions(shard_index, tok_dev, stride, offset, row_count):
    return (
        shard_index * tok_dev
        + stride * jnp.arange(row_count, dtype=jnp.int32)[None, :]
        + offset[:, None]
    )


def window_positions(shard_index, distances, tok_dev, stride, offset, row_count):
    return jnp.concatenate(
        [row_positions(shard_index + d, tok_dev, stride, offset, row_count) for d in distances],
        axis=1,
    )


def dot_nt(left, right):
    return lax.dot_general(
        left, right, (((1,), (1,)), ((), ())), preferred_element_type=jnp.float32
    )


def dot_nn(left, right):
    return lax.dot_general(
        left, right, (((1,), (0,)), ((), ())), preferred_element_type=jnp.float32
    )


def attend_rows(q, g, parts, scale):
    scored = [
        (k, v, live, jnp.where(live, dot_nt(q, k) * scale, VERY_NEGATIVE))
        for k, v, live in parts
    ]
    top = None
    for k, v, live, scores in scored:
        part_top = jnp.max(scores, axis=1, keepdims=True)
        top = part_top if top is None else jnp.maximum(top, part_top)
    total = None
    numer = None
    weights = []
    for k, v, live, scores in scored:
        w = jnp.where(live, jnp.exp(scores - top), 0.0)
        part_total = jnp.sum(w, axis=1, keepdims=True)
        part_numer = dot_nn(w.astype(jnp.bfloat16), v)
        total = part_total if total is None else total + part_total
        numer = part_numer if numer is None else numer + part_numer
        weights.append(w)
    attended = numer / total
    delta = jnp.sum(g.astype(jnp.float32) * attended, axis=1, keepdims=True)
    inverse = 1.0 / total
    grad_query = None
    for (k, v, live, scores), w in zip(scored, weights):
        probability = w * inverse
        grad_probs = dot_nt(g, v)
        grad_scores = (probability * (grad_probs - delta)).astype(jnp.bfloat16)
        part = dot_nn(grad_scores, k) * scale
        grad_query = part if grad_query is None else grad_query + part
    return grad_query, top, inverse, delta


def query_kernel(*refs, scale, n_short):
    q_ref, g_ref, qpos_ref, qss_ref, qsl_ref = refs[:5]
    shorts = [refs[5 + 4 * i : 9 + 4 * i] for i in range(n_short)]
    kl_ref, vl_ref, kpl_ref, ksl_ref = refs[5 + 4 * n_short : 9 + 4 * n_short]
    dq_ref, top_ref, inv_ref, delta_ref = refs[9 + 4 * n_short :]
    half = q_ref.shape[1] // 2
    for lo, hi, with_long in ((0, half, True), (half, 2 * half, False)):
        q = q_ref[0, lo:hi, :]
        g = g_ref[0, lo:hi, :]
        qpos = qpos_ref[0, lo:hi, :]
        qseg = qss_ref[0, lo:hi, :]
        parts = [
            (ks_ref[0], vs_ref[0], (kps_ref[0] <= qpos) & (kss_ref[0] == qseg))
            for ks_ref, vs_ref, kps_ref, kss_ref in shorts
        ]
        if with_long:
            parts.append(
                (kl_ref[0], vl_ref[0], (kpl_ref[0] <= qpos) & (ksl_ref[0] == qsl_ref[0, lo:hi, :]))
            )
        grad_query, top, inverse, delta = attend_rows(q, g, parts, scale)
        dq_ref[0, lo:hi, :] = grad_query.astype(dq_ref.dtype)
        top_ref[0, lo:hi, :] = top
        inv_ref[0, lo:hi, :] = inverse
        delta_ref[0, lo:hi, :] = delta


def key_rows(k, v, parts, scale):
    grad_key = None
    grad_value = None
    for q, g, live, stats in parts:
        scores = jnp.where(live, dot_nt(k, q) * scale, VERY_NEGATIVE)
        probability = jnp.where(live, jnp.exp(scores - stats[0:1, :]), 0.0) * stats[1:2, :]
        grad_probs = dot_nt(v, g)
        grad_scores = (probability * (grad_probs - stats[2:3, :])).astype(jnp.bfloat16)
        part_key = dot_nn(grad_scores, q) * scale
        part_value = dot_nn(probability.astype(jnp.bfloat16), g)
        grad_key = part_key if grad_key is None else grad_key + part_key
        grad_value = part_value if grad_value is None else grad_value + part_value
    return grad_key, grad_value


def key_kernel(
    k_ref, v_ref, qs_ref, gs_ref, ql_ref, gl_ref,
    kpos_ref, kss_ref, ksl_ref, qps_ref, qss_ref, sts_ref, qpl_ref, qsl_ref, stl_ref,
    dk_ref, dv_ref, *, scale,
):
    half = k_ref.shape[1] // 2
    qs = qs_ref[0]
    gs = gs_ref[0]
    sts = sts_ref[0]
    for lo, hi, with_long in ((0, half, True), (half, 2 * half, False)):
        k = k_ref[0, lo:hi, :]
        v = v_ref[0, lo:hi, :]
        kpos = kpos_ref[0, lo:hi, :]
        parts = [(qs, gs, (kpos <= qps_ref[0]) & (kss_ref[0, lo:hi, :] == qss_ref[0]), sts)]
        if with_long:
            parts.append(
                (
                    ql_ref[0],
                    gl_ref[0],
                    (kpos <= qpl_ref[0]) & (ksl_ref[0, lo:hi, :] == qsl_ref[0]),
                    stl_ref[0],
                )
            )
        grad_key, grad_value = key_rows(k, v, parts, scale)
        dk_ref[0, lo:hi, :] = grad_key.astype(dk_ref.dtype)
        dv_ref[0, lo:hi, :] = grad_value.astype(dv_ref.dtype)


def per_head(shape):
    return pl.BlockSpec((1,) + tuple(shape[1:]), lambda h: (h,) + (0,) * (len(shape) - 1))


def per_head_of(operand):
    if isinstance(operand, tuple):
        stacked, index = operand
        rest = (0,) * (stacked.ndim - 2)
        spec = pl.BlockSpec(
            (pl.Squeezed(), 1) + tuple(stacked.shape[2:]), lambda h: (index, h) + rest
        )
        return spec, stacked
    return per_head(operand.shape), operand


def run_per_head(kernel, inputs, out_shapes):
    heads = out_shapes[0].shape[0]
    specs, arrays = zip(*[per_head_of(x) for x in inputs])
    return pl.pallas_call(
        kernel,
        grid=(heads,),
        in_specs=list(specs),
        out_specs=[per_head(s.shape) for s in out_shapes],
        out_shape=out_shapes,
        compiler_params=pltpu.CompilerParams(dimension_semantics=("arbitrary",)),
    )(*arrays)


def column(x):
    return x[:, :, None]


def row(x):
    return x[:, None, :]


def shards(
    queries,
    key_vectors,
    value_vectors,
    grad_mixed,
    out_weight,
    head_phase,
    segments_short,
    segments_long,
):
    shard_index = lax.axis_index("seq")
    devices = lax.axis_size("seq")
    tok_dev = queries.shape[1]
    total = devices * tok_dev
    head_count = head_phase.shape[0]
    head_width = queries.shape[2] // head_count
    rows_short = tok_dev // 2
    rows_long = tok_dev // 4
    scale = 1.0 / math.sqrt(head_width)
    par_short = head_phase % 2
    par_long = head_phase // 2

    def split_rows(tensor):
        heads_major = jnp.transpose(tensor.reshape(tok_dev, head_count, head_width), (1, 0, 2))
        return take_rows(heads_major, par_short)

    def gathered(tensor):
        return lax.all_gather(tensor, "seq", axis=2, tiled=True)

    near_steps = [d for d in range(1, REACH_SHORT + 1) if d < devices]
    long_pos = row_positions(0, tok_dev, 4, head_phase, devices * rows_long)
    long_seg = segment_of(long_pos, segments_long)

    own_kv = jnp.stack([split_rows(key_vectors[0]), split_rows(value_vectors[0])])
    all_kv_long = gathered(take_rows(own_kv, par_long))
    near_kv = [own_kv] + [passed_along(own_kv, "seq", d) for d in near_steps]

    q_rows = split_rows(queries[0])
    core = shard_index % 2
    half_width = out_weight.shape[1] // 2
    own_half = lax.all_gather(
        lax.dynamic_slice_in_dim(out_weight, core * half_width, half_width, axis=1),
        "fsdp",
        axis=0,
        tiled=True,
    )
    other_half = lax.ppermute(own_half, "seq", [(i, i ^ 1) for i in range(devices)])
    grad_out = jnp.einsum(
        "td,rd->tr",
        lax.dynamic_slice_in_dim(grad_mixed[0], core * half_width, half_width, axis=1),
        own_half,
        preferred_element_type=jnp.float32,
    ) + jnp.einsum(
        "td,rd->tr",
        lax.dynamic_slice_in_dim(grad_mixed[0], (1 - core) * half_width, half_width, axis=1),
        other_half,
        preferred_element_type=jnp.float32,
    )
    grad_out = grad_out.astype(jnp.bfloat16)
    g_rows = split_rows(grad_out)
    own_qg = jnp.stack([q_rows, g_rows])
    all_qg_long = gathered(take_rows(own_qg, par_long))
    near_qg = [own_qg] + [passed_along(own_qg, "seq", -d) for d in near_steps]
    near_qg = jnp.concatenate(near_qg, axis=2)

    own_pos = row_positions(shard_index, tok_dev, 2, par_short, rows_short)
    own_seg_short = segment_of(own_pos, segments_short)
    own_is_long = (own_pos - head_phase[:, None]) % 4 == 0
    own_seg_long = jnp.where(own_is_long, segment_of(own_pos, segments_long), -3)

    short_keys = []
    for d, window in enumerate(near_kv):
        key_pos = row_positions(shard_index - d, tok_dev, 2, par_short, rows_short)
        key_seg = jnp.where(key_pos >= 0, segment_of(key_pos, segments_short), -1)
        short_keys += [(window, 0), (window, 1), row(key_pos), row(key_seg)]
    f32 = jnp.float32
    row_shape = jax.ShapeDtypeStruct((head_count, rows_short, head_width), jnp.bfloat16)
    stat_shape = jax.ShapeDtypeStruct((head_count, rows_short, 1), f32)
    grad_query, top, inverse, delta = run_per_head(
        functools.partial(query_kernel, scale=scale, n_short=len(near_kv)),
        [
            order_rows(q_rows, par_long),
            order_rows(g_rows, par_long),
            column(order_last(own_pos, par_long)),
            column(order_last(own_seg_short, par_long)),
            column(order_last(own_seg_long, par_long)),
        ]
        + short_keys
        + [(all_kv_long, 0), (all_kv_long, 1), row(long_pos), row(long_seg)],
        [row_shape, stat_shape, stat_shape, stat_shape],
    )
    grad_query = unorder_rows(grad_query, par_long)
    own_stats = unorder_last(
        jnp.stack([top[:, :, 0], inverse[:, :, 0], delta[:, :, 0]], axis=1), par_long
    )
    all_stats = lax.all_gather(own_stats, "seq", axis=2, tiled=True)
    all_stats_long = take_stats(all_stats, par_long)
    spare = jnp.zeros(own_stats.shape[:2] + (len(near_steps) * rows_short,), own_stats.dtype)
    near_stats = lax.dynamic_slice_in_dim(
        jnp.concatenate([all_stats, spare], axis=2),
        shard_index * rows_short,
        (len(near_steps) + 1) * rows_short,
        axis=2,
    )

    query_pos_short = window_positions(
        shard_index, list(range(len(near_steps) + 1)), tok_dev, 2, par_short, rows_short
    )
    query_seg_short = jnp.where(
        query_pos_short < total, segment_of(query_pos_short, segments_short), -2
    )
    ordered_kv = order_rows(own_kv, par_long)
    grad_key, grad_value = run_per_head(
        functools.partial(key_kernel, scale=scale),
        [
            (ordered_kv, 0),
            (ordered_kv, 1),
            (near_qg, 0),
            (near_qg, 1),
            (all_qg_long, 0),
            (all_qg_long, 1),
            column(order_last(own_pos, par_long)),
            column(order_last(own_seg_short, par_long)),
            column(order_last(own_seg_long, par_long)),
            row(query_pos_short),
            row(query_seg_short),
            near_stats,
            row(long_pos),
            row(long_seg),
            all_stats_long,
        ],
        [row_shape, row_shape],
    )
    grad_key = unorder_rows(grad_key, par_long)
    grad_value = unorder_rows(grad_value, par_long)

    def to_tokens(rows_here):
        tokens = put_rows(rows_here.astype(jnp.bfloat16), par_short)
        return jnp.transpose(tokens, (1, 0, 2)).reshape(1, tok_dev, head_count * head_width)

    return (to_tokens(grad_query), to_tokens(grad_key), to_tokens(grad_value))


def solution(mesh):
    placed = (
        P("fsdp", "seq", None),
        P("fsdp", "seq", None),
        P("fsdp", "seq", None),
        P("fsdp", "seq", None),
        P("fsdp", None),
        P(),
        P(),
        P(),
    )

    return jax.shard_map(
        shards,
        mesh=mesh,
        in_specs=placed,
        out_specs=(P("fsdp", "seq", None), P("fsdp", "seq", None), P("fsdp", "seq", None)),
        check_vma=False,
    )
```

profile of v0, /device:TPU:5, one launch (start us, length us, event | category | flops | bytes accessed | tf_op | source)
XLA Modules:
  0.0 383.2 jit_solution(14273359415443405668)
XLA Ops:
  7.3 2.5 constant_dynamic-slice_fusion
  9.8 34.5 %all-gather.4.cloned.1.call-done = bf16[1024,1024]{1,0:T(8,128)(2,1)} async-done(((bf16[512,1024]{1,0:T(8,128)(2,1)}), bf16[1024,1024]{1,0:T(8,128)(2,1)}) %all-gather.4.cloned.1.call-update) | async-done | bytes 2097168 | tf_op jit(solution)/shard_map/all_gather | solution.py:285
  45.4 0.9 copy-done.23
  48.8 0.9 copy.308
  53.2 2.9 fusion.2
  56.1 2.9 fusion
  61.8 1.4 broadcast_select_fusion
  67.0 1.5 compare_select_fusion.1
  68.5 1.4 broadcast_add_fusion.refs_27_.qpl_ref
  69.8 1.4 compare_convert_fusion.refs_28_.qsl_ref
  71.2 3.8 %bitcast_select_fusion.5 = (bf16[1,8,256,128]{3,2,1,0:T(8,128)(2,1)S(1)}, bf16[1,8,256,128]{3,2,1,0:T(8,128)(2,1)}, bf16[1,8,256,128]{3,2,1,0:T(8,128)(2,1)S(1)}, bf16[1,8,256,128]{3,2,1,0:T(8,128)(2,1)}) fusion(pred[8]{0:T(512)(128)(4,1)} %copy-done.30, bf16[8,256,1,128]{3,0,2,1:T(8,128)(2,1)S(1)} %copy-done.6, bf16[8,256,1,128]{3,0,2,1:T(8,128)(2,1)S(1)} %copy-done.4, ...), kind=kLoop, calls=%fused_computation.39 | loop fusion | flops 1048576 | bytes 6291464 | tf_op jit(solution)/shard_map/jit(_where)/select_n | solution.py:27
  75.1 1.8 pad_maximum_fusion.3
  76.9 2.0 collective-permute-start.5
  79.0 2.2 collective-permute-start.6
  81.2 1.9 collective-permute-start.7
  83.1 1.3 copy.254.refs_2_.kpos_ref
  84.5 1.3 copy.255.refs_3_.kss_ref
  85.8 1.3 copy.256.refs_4_.ksl_ref
  88.6 1.3 collective-permute-start.8
  89.9 1.3 pad_maximum_fusion.refs_5_.refs_6_
  91.2 5.6 %collective-permute-start.1 = (bf16[2,8,256,128]{3,2,1,0:T(8,128)(2,1)S(1)}, bf16[2,8,256,128]{3,2,1,0:T(8,128)(2,1)S(1)}, u32[]{:S(2)}, u32[]{:S(2)}) collective-permute-start(bf16[2,8,256,128]{3,2,1,0:T(8,128)(2,1)S(1)} %pad_maximum_fusion.refs_5_.refs_6_), channel_id=1, source_target_pairs={{0,2},{2,4},{4,6},{6,8},{8,10},{10,12},{12,14},{14,16},{16,18},{18... | collective-permute-start | bytes 3145736 | tf_op jit(solution)/shard_map/ppermute | solution.py:21
  97.1 30.9 %collective-permute-done.5 = bf16[2,8,256,128]{3,2,1,0:T(8,128)(2,1)} collective-permute-done((bf16[2,8,256,128]{3,2,1,0:T(8,128)(2,1)}, bf16[2,8,256,128]{3,2,1,0:T(8,128)(2,1)}, u32[]{:S(2)}, u32[]{:S(2)}) %collective-permute-start.5) | collective-permute-done | bytes 1048608 | tf_op jit(solution)/shard_map/ppermute | solution.py:21
  128.0 1.9 collective-permute-start.2
  129.9 65.1 %collective-permute-start.3 = (bf16[2,8,256,128]{3,2,1,0:T(8,128)(2,1)S(1)}, bf16[2,8,256,128]{3,2,1,0:T(8,128)(2,1)S(1)}, u32[]{:S(2)}, u32[]{:S(2)}) collective-permute-start(bf16[2,8,256,128]{3,2,1,0:T(8,128)(2,1)S(1)} %pad_maximum_fusion.refs_5_.refs_6_), channel_id=1, source_target_pairs={{0,6},{2,8},{4,10},{6,12},{8,14},{10,16},{12,18},{14,20},{16,22},{... | collective-permute-start | bytes 3145736 | tf_op jit(solution)/shard_map/ppermute | solution.py:21
  195.0 2.3 collective-permute-start.4
  197.3 1.1 pad_maximum_fusion.2.k_ref.v_ref
  198.6 1.1 pad_maximum_fusion.8
  199.7 2.4 constant_dynamic-update-slice_fusion.3
  202.1 2.4 constant_dynamic-update-slice_fusion.2
  204.5 2.5 constant_dynamic-update-slice_fusion.1
  207.0 1.2 constant_dynamic-update-slice_fusion.qs_ref.gs_ref
  208.2 10.5 %collective-permute-done.3.refs_17_.refs_18_ = bf16[2,8,256,128]{3,2,1,0:T(8,128)(2,1)S(1)} collective-permute-done((bf16[2,8,256,128]{3,2,1,0:T(8,128)(2,1)S(1)}, bf16[2,8,256,128]{3,2,1,0:T(8,128)(2,1)S(1)}, u32[]{:S(2)}, u32[]{:S(2)}) %collective-permute-start.3) | collective-permute-done | bytes 1048608 | tf_op jit(solution)/shard_map/ppermute | solution.py:21
  218.7 27.3 %collective-permute-done.4.refs_21_.refs_22_ = bf16[2,8,256,128]{3,2,1,0:T(8,128)(2,1)} collective-permute-done((bf16[2,8,256,128]{3,2,1,0:T(8,128)(2,1)S(1)}, bf16[2,8,256,128]{3,2,1,0:T(8,128)(2,1)}, u32[]{:S(2)}, u32[]{:S(2)}) %collective-permute-start.4) | collective-permute-done | bytes 1048608 | tf_op jit(solution)/shard_map/ppermute | solution.py:21
  246.1 24.8 %shard_map.103 = (bf16[8,256,128]{2,1,0:T(8,128)(2,1)}, f32[8,256,1]{2,1,0:T(8,128)}, f32[8,256,1]{2,1,0:T(8,128)}, f32[8,256,1]{2,1,0:T(8,128)}) custom-call(bf16[8,256,128]{2,1,0:T(8,128)(2,1)} %get-tuple-element.143.refs_0_, bf16[8,256,128]{2,1,0:T(8,128)(2,1)} %get-tuple-element.144.refs_1_, s32[8,256,1]{2,1,0:T(8,128)} %copy.254.refs_2_.kpos_ref, ...), custom_call_target="tpu_custom_call" | custom-call | tf_op jit(solution)/shard_map/pallas_call | solution.py:227
  270.9 1.8 reduce
  272.7 1.6 reduce.1
  275.1 38.2 %all_gather.15 = f32[8,3,4096]{2,1,0:T(4,128)S(1)} all-gather(f32[8,3,256]{2,1,0:T(4,128)S(1)} %copy.272), channel_id=1, replica_groups=mesh['seq'=16,'fsdp'=2] {'seq'}, dimensions={2}, use_global_device_ids=true | all-gather | bytes 417792 | tf_op jit(solution)/shard_map/all_gather | solution.py:340
  313.3 4.0 %copy.273 = f32[8,3,4096]{0,2,1:T(8,128)} copy(f32[8,3,4096]{2,1,0:T(4,128)S(1)} %all_gather.15) | data formatting | bytes 786432 | tf_op jit(solution)/shard_map/all_gather | solution.py:340
  317.3 11.0 %fusion.31 = (f32[8,3,2048,1]{0,3,2,1:T(1,128)}, f32[8,3,2048,1]{0,3,2,1:T(1,128)}) fusion(f32[8,3,2048,2]{0,3,2,1:T(2,128)} %bitcast.218), kind=kLoop, calls=%fused_computation.168 | loop fusion | bytes 786432 | tf_op jit(solution)/shard_map/slice | solution.py:40
  328.3 8.6 %copy.310 = f32[8,3,2048,1]{2,1,0,3:T(4,128)S(1)} copy(f32[8,3,2048,1]{0,3,2,1:T(1,128)} %get-tuple-element.24) | data formatting | bytes 393216
  336.8 8.6 %copy.311 = f32[8,3,2048,1]{2,1,0,3:T(4,128)S(1)} copy(f32[8,3,2048,1]{0,3,2,1:T(1,128)} %get-tuple-element.25) | data formatting | bytes 393216
  346.9 19.4 %shard_map.104 = (bf16[8,256,128]{2,1,0:T(8,128)(2,1)}, bf16[8,256,128]{2,1,0:T(8,128)(2,1)}) custom-call(bf16[2,8,256,128]{3,2,1,0:T(8,128)(2,1)} %pad_maximum_fusion.2.k_ref.v_ref, bf16[2,8,256,128]{3,2,1,0:T(8,128)(2,1)} %pad_maximum_fusion.2.k_ref.v_ref, bf16[2,8,1280,128]{3,2,1,0:T(8,128)(2,1)} %constant_dynamic-update-slice_fusion.qs_ref.gs_ref, ...), custom_call_target="tpu_custom_call" | custom-call | tf_op jit(solution)/shard_map/pallas_call | solution.py:227
  366.4 1.5 select_bitcast_fusion.9
  369.2 1.3 bitcast_select_fusion.7
  370.8 1.3 reshape.1284
  372.1 1.3 pad_maximum_fusion.4
  373.6 1.3 reshape.1282
  375.1 1.3 reshape.1279
  (161 shorter events, 19.2 us)
Async XLA Ops:
  7.2 46.0 %copy-start = (bf16[1,512,2048]{2,1,0:T(8,128)(2,1)S(1)}, bf16[1,512,2048]{2,1,0:T(8,128)(2,1)}, u32[]{:S(2)}) copy-start(bf16[1,512,2048]{2,1,0:T(8,128)(2,1)} %param.11) | copy-start | bytes 6291460
  7.2 37.9 %copy-start.22 = (bf16[1,512,1024]{2,1,0:T(8,128)(2,1)S(1)}, bf16[1,512,1024]{2,1,0:T(8,128)(2,1)}, u32[]{:S(2)}) copy-start(bf16[1,512,1024]{2,1,0:T(8,128)(2,1)} %param.9) | copy-start | bytes 3145732
  7.2 37.1 %all-gather.4.cloned.1.call-start = ((), (), s32[]{:S(2)}) async-start(), calls=%async_computation | async-start | bytes 3145728 | tf_op jit(solution)/shard_map/all_gather | solution.py:285
  9.7 236.3 %all-gather.6.cloned.1.call-start = ((), (), s32[]{:S(2)}) async-start(), calls=%async_computation.1 | async-start | bytes 8912896 | tf_op jit(solution)/shard_map/all_gather | solution.py:272
  44.3 11.8 %collective-permute-start = (bf16[1024,1024]{1,0:T(8,128)(2,1)}, bf16[1024,1024]{1,0:T(8,128)(2,1)}, u32[]{:S(2)}, u32[]{:S(2)}) collective-permute-start(bf16[1024,1024]{1,0:T(8,128)(2,1)} %all-gather.4.cloned.1.call-done), channel_id=1, source_target_pairs={{0,2},{2,0},{4,6},{6,4},{8,10},{10,8},{12,14},{14,12},{16,18},{18,... | collective-permute-start | bytes 6291464 | tf_op jit(solution)/shard_map/ppermute | solution.py:291
  45.1 1.2 copy-start.23
  47.0 3.6 copy-start.10
  47.0 3.6 copy-start.11
  47.0 3.6 copy-start.12
  47.0 3.6 copy-start.13
  47.0 3.6 copy-start.24
  50.9 1.1 copy-start.29
  51.0 0.8 copy-start.3
  51.0 1.0 copy-start.5
  52.6 7.6 %copy-start.30 = (pred[8]{0:T(512)(128)(4,1)}, pred[8]{0:T(512)(128)(4,1)S(1)}, u32[]{:S(2)}) copy-start(pred[8]{0:T(512)(128)(4,1)S(1)} %broadcast_compare_fusion.3) | copy-start | bytes 28
  59.3 1.1 copy-start.17
  59.3 1.6 copy-start.18
  59.3 1.7 copy-start.19
  59.3 1.9 copy-start.20
  59.4 0.8 copy-start.7
  59.4 2.4 copy-start.8
  61.8 2.2 copy-start.37
  63.3 8.0 %copy-start.4 = (bf16[8,256,1,128]{3,0,2,1:T(8,128)(2,1)S(1)}, bf16[8,256,1,128]{3,0,2,1:T(8,128)(2,1)}, u32[]{:S(2)}) copy-start(bf16[8,256,1,128]{3,0,2,1:T(8,128)(2,1)} %copy-done.3) | copy-start | bytes 1572868
  63.3 8.0 %copy-start.6 = (bf16[8,256,1,128]{3,0,2,1:T(8,128)(2,1)S(1)}, bf16[8,256,1,128]{3,0,2,1:T(8,128)(2,1)}, u32[]{:S(2)}) copy-start(bf16[8,256,1,128]{3,0,2,1:T(8,128)(2,1)} %copy-done.5) | copy-start | bytes 1572868
  63.3 283.7 %all-gather.8.cloned.1.call-start = ((), (), s32[]{:S(2)}) async-start(), calls=%async_computation.2 | async-start | bytes 8912896 | tf_op jit(solution)/shard_map/all_gather | solution.py:272
  64.2 0.8 copy-start.32
  76.9 10.9 %copy-start.33 = (s32[7,1]{0,1:T(1,128)S(1)}, s32[7,1]{0,1:T(1,128)}, u32[]{:S(2)}) copy-start(s32[7,1]{0,1:T(1,128)} %copy-done.32) | copy-start | bytes 88
  76.9 51.0 %collective-permute-start.5 = (bf16[2,8,256,128]{3,2,1,0:T(8,128)(2,1)}, bf16[2,8,256,128]{3,2,1,0:T(8,128)(2,1)}, u32[]{:S(2)}, u32[]{:S(2)}) collective-permute-start(bf16[2,8,256,128]{3,2,1,0:T(8,128)(2,1)} %get-tuple-element.26), channel_id=1, source_target_pairs={{2,0},{4,2},{6,4},{8,6},{10,8},{12,10},{14,12},{16,14},{18,16},{20... | collective-permute-start | bytes 3145736 | tf_op jit(solution)/shard_map/ppermute | solution.py:21
  79.0 50.9 %collective-permute-start.6 = (bf16[2,8,256,128]{3,2,1,0:T(8,128)(2,1)}, bf16[2,8,256,128]{3,2,1,0:T(8,128)(2,1)}, u32[]{:S(2)}, u32[]{:S(2)}) collective-permute-start(bf16[2,8,256,128]{3,2,1,0:T(8,128)(2,1)} %get-tuple-element.26), channel_id=1, source_target_pairs={{4,0},{6,2},{8,4},{10,6},{12,8},{14,10},{16,12},{18,14},{20,16},{2... | collective-permute-start | bytes 3145736 | tf_op jit(solution)/shard_map/ppermute | solution.py:21
  81.2 113.8 %collective-permute-start.7 = (bf16[2,8,256,128]{3,2,1,0:T(8,128)(2,1)}, bf16[2,8,256,128]{3,2,1,0:T(8,128)(2,1)}, u32[]{:S(2)}, u32[]{:S(2)}) collective-permute-start(bf16[2,8,256,128]{3,2,1,0:T(8,128)(2,1)} %get-tuple-element.26), channel_id=1, source_target_pairs={{6,0},{8,2},{10,4},{12,6},{14,8},{16,10},{18,12},{20,14},{22,16},{... | collective-permute-start | bytes 3145736 | tf_op jit(solution)/shard_map/ppermute | solution.py:21
  84.5 12.3 %copy-start.31 = (pred[8]{0:T(512)(128)(4,1)S(1)}, pred[8]{0:T(512)(128)(4,1)}, u32[]{:S(2)}) copy-start(pred[8]{0:T(512)(128)(4,1)} %copy-done.30) | copy-start | bytes 28
  88.6 118.4 %collective-permute-start.8 = (bf16[2,8,256,128]{3,2,1,0:T(8,128)(2,1)}, bf16[2,8,256,128]{3,2,1,0:T(8,128)(2,1)S(1)}, u32[]{:S(2)}, u32[]{:S(2)}) collective-permute-start(bf16[2,8,256,128]{3,2,1,0:T(8,128)(2,1)} %get-tuple-element.26), channel_id=1, source_target_pairs={{8,0},{10,2},{12,4},{14,6},{16,8},{18,10},{20,12},{22,14},{24,16},... | collective-permute-start | bytes 3145736 | tf_op jit(solution)/shard_map/ppermute | solution.py:21
  91.2 107.3 %copy-start.2 = (bf16[2,8,256,128]{3,2,1,0:T(8,128)(2,1)}, bf16[2,8,256,128]{3,2,1,0:T(8,128)(2,1)S(1)}, u32[]{:S(2)}) copy-start(bf16[2,8,256,128]{3,2,1,0:T(8,128)(2,1)S(1)} %pad_maximum_fusion.refs_5_.refs_6_) | copy-start | bytes 3145732
  91.2 106.1 %copy-start.9 = (bf16[2,8,128,128]{3,2,1,0:T(8,128)(2,1)S(1)}, bf16[2,8,128,128]{3,2,1,0:T(8,128)(2,1)}, u32[]{:S(2)}) copy-start(bf16[2,8,128,128]{3,2,1,0:T(8,128)(2,1)} %get-tuple-element.29) | copy-start | bytes 1572868
  91.2 106.1 %copy-start.21 = (bf16[2,8,128,128]{3,2,1,0:T(8,128)(2,1)S(1)}, bf16[2,8,128,128]{3,2,1,0:T(8,128)(2,1)}, u32[]{:S(2)}) copy-start(bf16[2,8,128,128]{3,2,1,0:T(8,128)(2,1)} %get-tuple-element.28) | copy-start | bytes 1572868
  91.2 116.9 %collective-permute-start.1 = (bf16[2,8,256,128]{3,2,1,0:T(8,128)(2,1)S(1)}, bf16[2,8,256,128]{3,2,1,0:T(8,128)(2,1)S(1)}, u32[]{:S(2)}, u32[]{:S(2)}) collective-permute-start(bf16[2,8,256,128]{3,2,1,0:T(8,128)(2,1)S(1)} %pad_maximum_fusion.refs_5_.refs_6_), channel_id=1, source_target_pairs={{0,2},{2,4},{4,6},{6,8},{8,10},{10,12},{12,14},{14,16},{16,18},{18... | collective-permute-start | bytes 3145736 | tf_op jit(solution)/shard_map/ppermute | solution.py:21
  128.0 80.2 %collective-permute-start.2 = (bf16[2,8,256,128]{3,2,1,0:T(8,128)(2,1)S(1)}, bf16[2,8,256,128]{3,2,1,0:T(8,128)(2,1)S(1)}, u32[]{:S(2)}, u32[]{:S(2)}) collective-permute-start(bf16[2,8,256,128]{3,2,1,0:T(8,128)(2,1)S(1)} %pad_maximum_fusion.refs_5_.refs_6_), channel_id=1, source_target_pairs={{0,4},{2,6},{4,8},{6,10},{8,12},{10,14},{12,16},{14,18},{16,20},{1... | collective-permute-start | bytes 3145736 | tf_op jit(solution)/shard_map/ppermute | solution.py:21
  129.9 88.8 %collective-permute-start.3 = (bf16[2,8,256,128]{3,2,1,0:T(8,128)(2,1)S(1)}, bf16[2,8,256,128]{3,2,1,0:T(8,128)(2,1)S(1)}, u32[]{:S(2)}, u32[]{:S(2)}) collective-permute-start(bf16[2,8,256,128]{3,2,1,0:T(8,128)(2,1)S(1)} %pad_maximum_fusion.refs_5_.refs_6_), channel_id=1, source_target_pairs={{0,6},{2,8},{4,10},{6,12},{8,14},{10,16},{12,18},{14,20},{16,22},{... | collective-permute-start | bytes 3145736 | tf_op jit(solution)/shard_map/ppermute | solution.py:21
  195.0 51.0 %collective-permute-start.4 = (bf16[2,8,256,128]{3,2,1,0:T(8,128)(2,1)S(1)}, bf16[2,8,256,128]{3,2,1,0:T(8,128)(2,1)}, u32[]{:S(2)}, u32[]{:S(2)}) collective-permute-start(bf16[2,8,256,128]{3,2,1,0:T(8,128)(2,1)S(1)} %pad_maximum_fusion.refs_5_.refs_6_), channel_id=1, source_target_pairs={{0,8},{2,10},{4,12},{6,14},{8,16},{10,18},{12,20},{14,22},{16,24},... | collective-permute-start | bytes 3145736 | tf_op jit(solution)/shard_map/ppermute | solution.py:21
  208.2 10.5 %copy-start.14 = (bf16[2,8,256,128]{3,2,1,0:T(8,128)(2,1)}, bf16[2,8,256,128]{3,2,1,0:T(8,128)(2,1)S(1)}, u32[]{:S(2)}) copy-start(bf16[2,8,256,128]{3,2,1,0:T(8,128)(2,1)S(1)} %collective-permute-done.1.refs_9_.refs_10_) | copy-start | bytes 3145732
  208.2 37.9 %copy-start.15 = (bf16[2,8,256,128]{3,2,1,0:T(8,128)(2,1)}, bf16[2,8,256,128]{3,2,1,0:T(8,128)(2,1)S(1)}, u32[]{:S(2)}) copy-start(bf16[2,8,256,128]{3,2,1,0:T(8,128)(2,1)S(1)} %collective-permute-done.2.refs_13_.refs_14_) | copy-start | bytes 3145732
  218.7 27.4 %copy-start.16 = (bf16[2,8,256,128]{3,2,1,0:T(8,128)(2,1)}, bf16[2,8,256,128]{3,2,1,0:T(8,128)(2,1)S(1)}, u32[]{:S(2)}) copy-start(bf16[2,8,256,128]{3,2,1,0:T(8,128)(2,1)S(1)} %collective-permute-done.3.refs_17_.refs_18_) | copy-start | bytes 3145732
  270.9 3.4 copy-start.25
  346.9 19.5 %copy-start.26 = (bf16[8,256,128]{2,1,0:T(8,128)(2,1)S(1)}, bf16[8,256,128]{2,1,0:T(8,128)(2,1)}, u32[]{:S(2)}) copy-start(bf16[8,256,128]{2,1,0:T(8,128)(2,1)} %get-tuple-element.9) | copy-start | bytes 1572868
  346.9 19.5 %copy-start.35 = (pred[8]{0:T(512)(128)(4,1)S(1)}, pred[8]{0:T(512)(128)(4,1)}, u32[]{:S(2)}) copy-start(pred[8]{0:T(512)(128)(4,1)} %get-tuple-element.141) | copy-start | bytes 28
  346.9 19.5 %copy-start.36 = (pred[8]{0:T(512)(128)(4,1)S(1)}, pred[8]{0:T(512)(128)(4,1)}, u32[]{:S(2)}) copy-start(pred[8]{0:T(512)(128)(4,1)} %get-tuple-element.139) | copy-start | bytes 28
  368.4 0.8 copy-start.34
  374.9 1.8 copy-start.1
  (2 other events, 1.1 us)
Sparse Core Ops, SparseCore 0:
  10.1 34.1 all-gather.3
  63.4 129.2 all-gather.5
  194.9 92.0 all-gather.7
where the time goes:
time: 389 us; the launch traced here: 383 us
  waiting for transfers between devices  104 us (27%)
  starting transfers between devices  83.2 us (21%)
  local copies, waits for them, and re-layouts  64 us (16%)
  Pallas kernels  44.3 us (11%)
  blocking collectives  38.2 us (10%)
  other arithmetic  28.4 us (7%)
  between operations  15.2 us (4%)
  matrix products  5.78 us (1%)
    ppermute x8, starting transfers between devices, passed_along(): return lax.ppermute(value, axis, pairs)  82.3 us
    ppermute x8, waiting for transfers between devices, passed_along(): return lax.ppermute(value, axis, pairs)  68.8 us
    pallas_call x2, Pallas kernels, run_per_head(): pl.pallas_call(kernel, grid=(heads,), in_specs=list(specs), out_specs=[pe...  44.3 us
    all_gather x1, blocking collectives, shards(): all_stats = lax.all_gather(own_stats, 'seq', axis=2, tiled=True)  38.2 us
    all_gather x1, waiting for transfers between devices, shards(): lax.all_gather(lax.dynamic_slice_in_dim(out_weight, core * half_width, ha...  34.5 us
    unnamed x99, local copies, waits for them, and re-layouts  33.5 us
    slice x1, local copies, waits for them, and re-layouts, take_stats(): paired[..., 0]  11 us
  transfers between devices with their start and end apart: 12, of which 4 were waited for; matrix products, arithmetic and copies ran while one was open for 20% of the time, Pallas kernels for 6%

commit v1 on v0

--- a/solution.py
+++ b/solution.py
@@ -337,15 +337,11 @@
     own_stats = unorder_last(
         jnp.stack([top[:, :, 0], inverse[:, :, 0], delta[:, :, 0]], axis=1), par_long
     )
-    all_stats = lax.all_gather(own_stats, "seq", axis=2, tiled=True)
-    all_stats_long = take_stats(all_stats, par_long)
-    spare = jnp.zeros(own_stats.shape[:2] + (len(near_steps) * rows_short,), own_stats.dtype)
-    near_stats = lax.dynamic_slice_in_dim(
-        jnp.concatenate([all_stats, spare], axis=2),
-        shard_index * rows_short,
-        (len(near_steps) + 1) * rows_short,
-        axis=2,
-    )
+    near_stats = [own_stats] + [passed_along(own_stats, "seq", -d) for d in near_steps]
+    near_stats = jnp.concatenate(near_stats, axis=2)
+    all_stats_long = lax.all_gather(
+        take_stats(own_stats, par_long).reshape(3 * head_count, rows_long), "seq", axis=1, tiled=True
+    ).reshape(head_count, 3, devices * rows_long)
 
     query_pos_short = window_positions(
         shard_index, list(range(len(near_steps) + 1)), tok_dev, 2, par_short, rows_short

time: 389 us -> 367 us (0.943)
  local copies, waits for them, and re-layouts: 64 us -> 32.9 us
  starting transfers between devices: 83.2 us -> 94.5 us
    unnamed x99 -> x103, local copies, waits for them, and re-layouts: 33.5 us -> 17.1 us
    ppermute x8 -> x12, starting transfers between devices: 82.3 us -> 93.6 us  [passed_along(): return lax.ppermute(value, axis, pairs)]
    slice x1, local copies, waits for them, and re-layouts: 11 us -> 0.01 us  [take_stats(): paired[..., 0]]
    all_gather x1 -> x0, local copies, waits for them, and re-layouts: 4 us -> none  [shards(): all_stats = lax.all_gather(own_stats, 'seq', axis=2, tiled=True)]
    ppermute x8 -> x12, waiting for transfers between devices: 68.8 us -> 68 us  [passed_along(): return lax.ppermute(value, axis, pairs)]
  transfers between devices with their start and end apart: 12 -> 16, of which waited for: 4 -> 4; matrix products, arithmetic and copies ran while one was open for 20% -> 12% of each run, Pallas kernels for 6% -> 7%
where the time goes in v1:
time: 367 us; the launch traced here: 362 us
  waiting for transfers between devices  103 us (28%)
  starting transfers between devices  94.5 us (26%)
  Pallas kernels  44.1 us (12%)
  blocking collectives  38.4 us (10%)
  local copies, waits for them, and re-layouts  32.9 us (9%)
  other arithmetic  27.6 us (8%)
  between operations  15.4 us (4%)
  matrix products  5.78 us (2%)
    ppermute x12, starting transfers between devices, passed_along(): return lax.ppermute(value, axis, pairs)  93.6 us
    ppermute x12, waiting for transfers between devices, passed_along(): return lax.ppermute(value, axis, pairs)  68 us
    pallas_call x2, Pallas kernels, run_per_head(): pl.pallas_call(kernel, grid=(heads,), in_specs=list(specs), out_specs=[pe...  44.1 us
    all_gather x1, blocking collectives, shards(): lax.all_gather(take_stats(own_stats, par_long).reshape(3 * head_count, ro...  38.4 us
    all_gather x1, waiting for transfers between devices, shards(): lax.all_gather(lax.dynamic_slice_in_dim(out_weight, core * half_width, ha...  34.5 us
    unnamed x103, local copies, waits for them, and re-layouts  17.1 us
  transfers between devices with their start and end apart: 16, of which 4 were waited for; matrix products, arithmetic and copies ran while one was open for 12% of the time, Pallas kernels for 7%

profile of v1, /device:TPU:5, one launch (start us, length us, event | category | flops | bytes accessed | tf_op | source)
XLA Modules:
  0.0 362.0 jit_solution(11866500292830976414)
XLA Ops:
  7.3 2.5 constant_dynamic-slice_fusion
  9.8 34.5 %all-gather.4.cloned.1.call-done = bf16[1024,1024]{1,0:T(8,128)(2,1)} async-done(((bf16[512,1024]{1,0:T(8,128)(2,1)}), bf16[1024,1024]{1,0:T(8,128)(2,1)}) %all-gather.4.cloned.1.call-update) | async-done | bytes 2097168 | tf_op jit(solution)/shard_map/all_gather | solution.py:285
  45.4 0.9 copy-done.23
  48.8 0.9 copy.323
  53.2 2.9 fusion.2
  56.1 2.9 fusion
  61.9 1.4 broadcast_select_fusion
  67.0 1.4 compare_select_fusion.1
  68.4 1.4 broadcast_add_fusion.refs_27_.qpl_ref
  69.7 1.4 compare_convert_fusion.refs_28_.qsl_ref
  71.1 3.8 %bitcast_select_fusion.5 = (bf16[1,8,256,128]{3,2,1,0:T(8,128)(2,1)S(1)}, bf16[1,8,256,128]{3,2,1,0:T(8,128)(2,1)}, bf16[1,8,256,128]{3,2,1,0:T(8,128)(2,1)S(1)}, bf16[1,8,256,128]{3,2,1,0:T(8,128)(2,1)}) fusion(pred[8]{0:T(512)(128)(4,1)} %copy-done.31, bf16[8,256,1,128]{3,0,2,1:T(8,128)(2,1)S(1)} %copy-done.6, bf16[8,256,1,128]{3,0,2,1:T(8,128)(2,1)S(1)} %copy-done.4, ...), kind=kLoop, calls=%fused_computation.38 | loop fusion | flops 1048576 | bytes 6291464 | tf_op jit(solution)/shard_map/jit(_where)/select_n | solution.py:27
  74.9 1.8 pad_maximum_fusion.3
  76.8 2.0 collective-permute-start.5
  78.8 2.2 collective-permute-start.6
  81.0 1.9 collective-permute-start.7
  83.0 1.3 copy.266.refs_2_.kpos_ref
  84.3 1.3 copy.267.refs_3_.kss_ref
  85.7 1.3 copy.268.refs_4_.ksl_ref
  88.6 1.3 collective-permute-start.8
  89.9 1.3 pad_maximum_fusion.refs_5_.refs_6_
  91.2 5.6 %collective-permute-start.1 = (bf16[2,8,256,128]{3,2,1,0:T(8,128)(2,1)S(1)}, bf16[2,8,256,128]{3,2,1,0:T(8,128)(2,1)S(1)}, u32[]{:S(2)}, u32[]{:S(2)}) collective-permute-start(bf16[2,8,256,128]{3,2,1,0:T(8,128)(2,1)S(1)} %pad_maximum_fusion.refs_5_.refs_6_), channel_id=1, source_target_pairs={{0,2},{2,4},{4,6},{6,8},{8,10},{10,12},{12,14},{14,16},{16,18},{18... | collective-permute-start | bytes 3145736 | tf_op jit(solution)/shard_map/ppermute | solution.py:21
  97.1 30.3 %collective-permute-done.5 = bf16[2,8,256,128]{3,2,1,0:T(8,128)(2,1)} collective-permute-done((bf16[2,8,256,128]{3,2,1,0:T(8,128)(2,1)}, bf16[2,8,256,128]{3,2,1,0:T(8,128)(2,1)}, u32[]{:S(2)}, u32[]{:S(2)}) %collective-permute-start.5) | collective-permute-done | bytes 1048608 | tf_op jit(solution)/shard_map/ppermute | solution.py:21
  127.4 1.9 collective-permute-start.2
  129.3 65.5 %collective-permute-start.3 = (bf16[2,8,256,128]{3,2,1,0:T(8,128)(2,1)S(1)}, bf16[2,8,256,128]{3,2,1,0:T(8,128)(2,1)S(1)}, u32[]{:S(2)}, u32[]{:S(2)}) collective-permute-start(bf16[2,8,256,128]{3,2,1,0:T(8,128)(2,1)S(1)} %pad_maximum_fusion.refs_5_.refs_6_), channel_id=1, source_target_pairs={{0,6},{2,8},{4,10},{6,12},{8,14},{10,16},{12,18},{14,20},{16,22},{... | collective-permute-start | bytes 3145736 | tf_op jit(solution)/shard_map/ppermute | solution.py:21
  194.8 2.4 collective-permute-start.4
  197.2 1.1 pad_maximum_fusion.2.k_ref.v_ref
  198.5 1.1 pad_maximum_fusion.8
  199.5 2.5 constant_dynamic-update-slice_fusion.3
  202.0 2.5 constant_dynamic-update-slice_fusion.2
  204.5 2.5 constant_dynamic-update-slice_fusion.1
  206.9 1.2 constant_dynamic-update-slice_fusion.qs_ref.gs_ref
  208.2 10.1 %collective-permute-done.3.refs_17_.refs_18_ = bf16[2,8,256,128]{3,2,1,0:T(8,128)(2,1)S(1)} collective-permute-done((bf16[2,8,256,128]{3,2,1,0:T(8,128)(2,1)S(1)}, bf16[2,8,256,128]{3,2,1,0:T(8,128)(2,1)S(1)}, u32[]{:S(2)}, u32[]{:S(2)}) %collective-permute-start.3) | collective-permute-done | bytes 1048608 | tf_op jit(solution)/shard_map/ppermute | solution.py:21
  218.2 27.6 %collective-permute-done.4.refs_21_.refs_22_ = bf16[2,8,256,128]{3,2,1,0:T(8,128)(2,1)} collective-permute-done((bf16[2,8,256,128]{3,2,1,0:T(8,128)(2,1)S(1)}, bf16[2,8,256,128]{3,2,1,0:T(8,128)(2,1)}, u32[]{:S(2)}, u32[]{:S(2)}) %collective-permute-start.4) | collective-permute-done | bytes 1048608 | tf_op jit(solution)/shard_map/ppermute | solution.py:21
  245.9 24.7 %shard_map.103 = (bf16[8,256,128]{2,1,0:T(8,128)(2,1)}, f32[8,256,1]{2,1,0:T(8,128)}, f32[8,256,1]{2,1,0:T(8,128)}, f32[8,256,1]{2,1,0:T(8,128)}) custom-call(bf16[8,256,128]{2,1,0:T(8,128)(2,1)} %get-tuple-element.143.refs_0_, bf16[8,256,128]{2,1,0:T(8,128)(2,1)} %get-tuple-element.144.refs_1_, s32[8,256,1]{2,1,0:T(8,128)} %copy.266.refs_2_.kpos_ref, ...), custom_call_target="tpu_custom_call" | custom-call | tf_op jit(solution)/shard_map/pallas_call | solution.py:227
  270.6 1.9 reduce
  272.5 1.6 reduce.1
  274.9 1.9 collective-permute-start.9
  276.8 5.6 %collective-permute-start.10 = (f32[8,3,256]{2,1,0:T(4,128)S(1)}, f32[8,3,256]{2,1,0:T(4,128)S(1)}, u32[]{:S(2)}, u32[]{:S(2)}) collective-permute-start(f32[8,3,256]{2,1,0:T(4,128)S(1)} %copy.288), channel_id=1, source_target_pairs={{4,0},{6,2},{8,4},{10,6},{12,8},{14,10},{16,12},{18,14},{20,16},{2... | collective-permute-start | bytes 73736 | tf_op jit(solution)/shard_map/ppermute | solution.py:21
  282.4 1.9 collective-permute-start.11
  284.4 1.3 collective-permute-start.12
  285.8 38.4 %all_gather.15 = f32[24,2048]{1,0:T(8,128)S(1)} all-gather(f32[24,128]{1,0:T(8,128)S(1)} %broadcast_select_fusion.6), channel_id=1, replica_groups=mesh['seq'=16,'fsdp'=2] {'seq'}, dimensions={1}, use_global_device_ids=true | all-gather | bytes 208896 | tf_op jit(solution)/shard_map/all_gather | solution.py:342
  325.8 19.4 %shard_map.104 = (bf16[8,256,128]{2,1,0:T(8,128)(2,1)}, bf16[8,256,128]{2,1,0:T(8,128)(2,1)}) custom-call(bf16[2,8,256,128]{3,2,1,0:T(8,128)(2,1)} %pad_maximum_fusion.2.k_ref.v_ref, bf16[2,8,256,128]{3,2,1,0:T(8,128)(2,1)} %pad_maximum_fusion.2.k_ref.v_ref, bf16[2,8,1280,128]{3,2,1,0:T(8,128)(2,1)} %constant_dynamic-update-slice_fusion.qs_ref.gs_ref, ...), custom_call_target="tpu_custom_call" | custom-call | tf_op jit(solution)/shard_map/pallas_call | solution.py:227
  345.2 1.5 select_bitcast_fusion.9
  348.0 1.3 bitcast_select_fusion.7
  349.6 1.3 reshape.1289
  350.9 1.3 pad_maximum_fusion.4
  352.4 1.3 reshape.1287
  353.9 1.3 reshape.1284
  (179 shorter events, 19.3 us)
Async XLA Ops:
  7.2 46.0 %copy-start = (bf16[1,512,2048]{2,1,0:T(8,128)(2,1)S(1)}, bf16[1,512,2048]{2,1,0:T(8,128)(2,1)}, u32[]{:S(2)}) copy-start(bf16[1,512,2048]{2,1,0:T(8,128)(2,1)} %param.11) | copy-start | bytes 6291460
  7.2 37.9 %copy-start.22 = (bf16[1,512,1024]{2,1,0:T(8,128)(2,1)S(1)}, bf16[1,512,1024]{2,1,0:T(8,128)(2,1)}, u32[]{:S(2)}) copy-start(bf16[1,512,1024]{2,1,0:T(8,128)(2,1)} %param.9) | copy-start | bytes 3145732
  7.2 37.1 %all-gather.4.cloned.1.call-start = ((), (), s32[]{:S(2)}) async-start(), calls=%async_computation | async-start | bytes 3145728 | tf_op jit(solution)/shard_map/all_gather | solution.py:285
  9.7 236.1 %all-gather.6.cloned.1.call-start = ((), (), s32[]{:S(2)}) async-start(), calls=%async_computation.1 | async-start | bytes 8912896 | tf_op jit(solution)/shard_map/all_gather | solution.py:272
  44.3 11.8 %collective-permute-start = (bf16[1024,1024]{1,0:T(8,128)(2,1)}, bf16[1024,1024]{1,0:T(8,128)(2,1)}, u32[]{:S(2)}, u32[]{:S(2)}) collective-permute-start(bf16[1024,1024]{1,0:T(8,128)(2,1)} %all-gather.4.cloned.1.call-done), channel_id=1, source_target_pairs={{0,2},{2,0},{4,6},{6,4},{8,10},{10,8},{12,14},{14,12},{16,18},{18,... | collective-permute-start | bytes 6291464 | tf_op jit(solution)/shard_map/ppermute | solution.py:291
  45.1 1.2 copy-start.23
  47.0 3.6 copy-start.10
  47.0 3.6 copy-start.11
  47.0 3.6 copy-start.12
  47.0 3.6 copy-start.13
  47.0 3.6 copy-start.24
  50.9 1.1 copy-start.30
  51.0 1.0 copy-start.5
  52.7 7.7 %copy-start.31 = (pred[8]{0:T(512)(128)(4,1)}, pred[8]{0:T(512)(128)(4,1)S(1)}, u32[]{:S(2)}) copy-start(pred[8]{0:T(512)(128)(4,1)S(1)} %broadcast_compare_fusion.3) | copy-start | bytes 28
  59.3 1.1 copy-start.17
  59.3 1.6 copy-start.18
  59.3 1.7 copy-start.19
  59.3 1.9 copy-start.20
  59.4 2.4 copy-start.8
  61.9 2.2 copy-start.38
  63.3 7.9 %copy-start.4 = (bf16[8,256,1,128]{3,0,2,1:T(8,128)(2,1)S(1)}, bf16[8,256,1,128]{3,0,2,1:T(8,128)(2,1)}, u32[]{:S(2)}) copy-start(bf16[8,256,1,128]{3,0,2,1:T(8,128)(2,1)} %copy-done.3) | copy-start | bytes 1572868
  63.3 7.9 %copy-start.6 = (bf16[8,256,1,128]{3,0,2,1:T(8,128)(2,1)S(1)}, bf16[8,256,1,128]{3,0,2,1:T(8,128)(2,1)}, u32[]{:S(2)}) copy-start(bf16[8,256,1,128]{3,0,2,1:T(8,128)(2,1)} %copy-done.5) | copy-start | bytes 1572868
  63.3 261.9 %all-gather.8.cloned.1.call-start = ((), (), s32[]{:S(2)}) async-start(), calls=%async_computation.2 | async-start | bytes 8912896 | tf_op jit(solution)/shard_map/all_gather | solution.py:272
  76.8 11.1 %copy-start.34 = (s32[7,1]{0,1:T(1,128)S(1)}, s32[7,1]{0,1:T(1,128)}, u32[]{:S(2)}) copy-start(s32[7,1]{0,1:T(1,128)} %copy-done.33) | copy-start | bytes 88
  76.8 50.6 %collective-permute-start.5 = (bf16[2,8,256,128]{3,2,1,0:T(8,128)(2,1)}, bf16[2,8,256,128]{3,2,1,0:T(8,128)(2,1)}, u32[]{:S(2)}, u32[]{:S(2)}) collective-permute-start(bf16[2,8,256,128]{3,2,1,0:T(8,128)(2,1)} %get-tuple-element.24), channel_id=1, source_target_pairs={{2,0},{4,2},{6,4},{8,6},{10,8},{12,10},{14,12},{16,14},{18,16},{20... | collective-permute-start | bytes 3145736 | tf_op jit(solution)/shard_map/ppermute | solution.py:21
  78.8 50.5 %collective-permute-start.6 = (bf16[2,8,256,128]{3,2,1,0:T(8,128)(2,1)}, bf16[2,8,256,128]{3,2,1,0:T(8,128)(2,1)}, u32[]{:S(2)}, u32[]{:S(2)}) collective-permute-start(bf16[2,8,256,128]{3,2,1,0:T(8,128)(2,1)} %get-tuple-element.24), channel_id=1, source_target_pairs={{4,0},{6,2},{8,4},{10,6},{12,8},{14,10},{16,12},{18,14},{20,16},{2... | collective-permute-start | bytes 3145736 | tf_op jit(solution)/shard_map/ppermute | solution.py:21
  81.0 113.8 %collective-permute-start.7 = (bf16[2,8,256,128]{3,2,1,0:T(8,128)(2,1)}, bf16[2,8,256,128]{3,2,1,0:T(8,128)(2,1)}, u32[]{:S(2)}, u32[]{:S(2)}) collective-permute-start(bf16[2,8,256,128]{3,2,1,0:T(8,128)(2,1)} %get-tuple-element.24), channel_id=1, source_target_pairs={{6,0},{8,2},{10,4},{12,6},{14,8},{16,10},{18,12},{20,14},{22,16},{... | collective-permute-start | bytes 3145736 | tf_op jit(solution)/shard_map/ppermute | solution.py:21
  84.3 12.5 %copy-start.32 = (pred[8]{0:T(512)(128)(4,1)S(1)}, pred[8]{0:T(512)(128)(4,1)}, u32[]{:S(2)}) copy-start(pred[8]{0:T(512)(128)(4,1)} %copy-done.31) | copy-start | bytes 28
  88.6 118.3 %collective-permute-start.8 = (bf16[2,8,256,128]{3,2,1,0:T(8,128)(2,1)}, bf16[2,8,256,128]{3,2,1,0:T(8,128)(2,1)S(1)}, u32[]{:S(2)}, u32[]{:S(2)}) collective-permute-start(bf16[2,8,256,128]{3,2,1,0:T(8,128)(2,1)} %get-tuple-element.24), channel_id=1, source_target_pairs={{8,0},{10,2},{12,4},{14,6},{16,8},{18,10},{20,12},{22,14},{24,16},... | collective-permute-start | bytes 3145736 | tf_op jit(solution)/shard_map/ppermute | solution.py:21
  91.2 107.1 %copy-start.2 = (bf16[2,8,256,128]{3,2,1,0:T(8,128)(2,1)}, bf16[2,8,256,128]{3,2,1,0:T(8,128)(2,1)S(1)}, u32[]{:S(2)}) copy-start(bf16[2,8,256,128]{3,2,1,0:T(8,128)(2,1)S(1)} %pad_maximum_fusion.refs_5_.refs_6_) | copy-start | bytes 3145732
  91.2 106.0 %copy-start.9 = (bf16[2,8,128,128]{3,2,1,0:T(8,128)(2,1)S(1)}, bf16[2,8,128,128]{3,2,1,0:T(8,128)(2,1)}, u32[]{:S(2)}) copy-start(bf16[2,8,128,128]{3,2,1,0:T(8,128)(2,1)} %get-tuple-element.27) | copy-start | bytes 1572868
  91.2 106.0 %copy-start.21 = (bf16[2,8,128,128]{3,2,1,0:T(8,128)(2,1)S(1)}, bf16[2,8,128,128]{3,2,1,0:T(8,128)(2,1)}, u32[]{:S(2)}) copy-start(bf16[2,8,128,128]{3,2,1,0:T(8,128)(2,1)} %get-tuple-element.26) | copy-start | bytes 1572868
  91.2 116.9 %collective-permute-start.1 = (bf16[2,8,256,128]{3,2,1,0:T(8,128)(2,1)S(1)}, bf16[2,8,256,128]{3,2,1,0:T(8,128)(2,1)S(1)}, u32[]{:S(2)}, u32[]{:S(2)}) collective-permute-start(bf16[2,8,256,128]{3,2,1,0:T(8,128)(2,1)S(1)} %pad_maximum_fusion.refs_5_.refs_6_), channel_id=1, source_target_pairs={{0,2},{2,4},{4,6},{6,8},{8,10},{10,12},{12,14},{14,16},{16,18},{18... | collective-permute-start | bytes 3145736 | tf_op jit(solution)/shard_map/ppermute | solution.py:21
  127.4 80.8 %collective-permute-start.2 = (bf16[2,8,256,128]{3,2,1,0:T(8,128)(2,1)S(1)}, bf16[2,8,256,128]{3,2,1,0:T(8,128)(2,1)S(1)}, u32[]{:S(2)}, u32[]{:S(2)}) collective-permute-start(bf16[2,8,256,128]{3,2,1,0:T(8,128)(2,1)S(1)} %pad_maximum_fusion.refs_5_.refs_6_), channel_id=1, source_target_pairs={{0,4},{2,6},{4,8},{6,10},{8,12},{10,14},{12,16},{14,18},{16,20},{1... | collective-permute-start | bytes 3145736 | tf_op jit(solution)/shard_map/ppermute | solution.py:21
  129.3 88.9 %collective-permute-start.3 = (bf16[2,8,256,128]{3,2,1,0:T(8,128)(2,1)S(1)}, bf16[2,8,256,128]{3,2,1,0:T(8,128)(2,1)S(1)}, u32[]{:S(2)}, u32[]{:S(2)}) collective-permute-start(bf16[2,8,256,128]{3,2,1,0:T(8,128)(2,1)S(1)} %pad_maximum_fusion.refs_5_.refs_6_), channel_id=1, source_target_pairs={{0,6},{2,8},{4,10},{6,12},{8,14},{10,16},{12,18},{14,20},{16,22},{... | collective-permute-start | bytes 3145736 | tf_op jit(solution)/shard_map/ppermute | solution.py:21
  194.8 51.0 %collective-permute-start.4 = (bf16[2,8,256,128]{3,2,1,0:T(8,128)(2,1)S(1)}, bf16[2,8,256,128]{3,2,1,0:T(8,128)(2,1)}, u32[]{:S(2)}, u32[]{:S(2)}) collective-permute-start(bf16[2,8,256,128]{3,2,1,0:T(8,128)(2,1)S(1)} %pad_maximum_fusion.refs_5_.refs_6_), channel_id=1, source_target_pairs={{0,8},{2,10},{4,12},{6,14},{8,16},{10,18},{12,20},{14,22},{16,24},... | collective-permute-start | bytes 3145736 | tf_op jit(solution)/shard_map/ppermute | solution.py:21
  208.2 10.1 %copy-start.14 = (bf16[2,8,256,128]{3,2,1,0:T(8,128)(2,1)}, bf16[2,8,256,128]{3,2,1,0:T(8,128)(2,1)S(1)}, u32[]{:S(2)}) copy-start(bf16[2,8,256,128]{3,2,1,0:T(8,128)(2,1)S(1)} %collective-permute-done.1.refs_9_.refs_10_) | copy-start | bytes 3145732
  208.2 37.7 %copy-start.15 = (bf16[2,8,256,128]{3,2,1,0:T(8,128)(2,1)}, bf16[2,8,256,128]{3,2,1,0:T(8,128)(2,1)S(1)}, u32[]{:S(2)}) copy-start(bf16[2,8,256,128]{3,2,1,0:T(8,128)(2,1)S(1)} %collective-permute-done.2.refs_13_.refs_14_) | copy-start | bytes 3145732
  218.2 27.6 %copy-start.16 = (bf16[2,8,256,128]{3,2,1,0:T(8,128)(2,1)}, bf16[2,8,256,128]{3,2,1,0:T(8,128)(2,1)S(1)}, u32[]{:S(2)}) copy-start(bf16[2,8,256,128]{3,2,1,0:T(8,128)(2,1)S(1)} %collective-permute-done.3.refs_17_.refs_18_) | copy-start | bytes 3145732
  270.6 3.5 copy-start.25
  274.9 50.1 %collective-permute-start.9 = (f32[8,3,256]{2,1,0:T(4,128)S(1)}, f32[8,3,256]{2,1,0:T(4,128)S(1)}, u32[]{:S(2)}, u32[]{:S(2)}) collective-permute-start(f32[8,3,256]{2,1,0:T(4,128)S(1)} %copy.288), channel_id=1, source_target_pairs={{2,0},{4,2},{6,4},{8,6},{10,8},{12,10},{14,12},{16,14},{18,16},{20... | collective-permute-start | bytes 73736 | tf_op jit(solution)/shard_map/ppermute | solution.py:21
  276.8 48.2 %collective-permute-start.10 = (f32[8,3,256]{2,1,0:T(4,128)S(1)}, f32[8,3,256]{2,1,0:T(4,128)S(1)}, u32[]{:S(2)}, u32[]{:S(2)}) collective-permute-start(f32[8,3,256]{2,1,0:T(4,128)S(1)} %copy.288), channel_id=1, source_target_pairs={{4,0},{6,2},{8,4},{10,6},{12,8},{14,10},{16,12},{18,14},{20,16},{2... | collective-permute-start | bytes 73736 | tf_op jit(solution)/shard_map/ppermute | solution.py:21
  282.4 42.6 %collective-permute-start.11 = (f32[8,3,256]{2,1,0:T(4,128)S(1)}, f32[8,3,256]{2,1,0:T(4,128)S(1)}, u32[]{:S(2)}, u32[]{:S(2)}) collective-permute-start(f32[8,3,256]{2,1,0:T(4,128)S(1)} %copy.288), channel_id=1, source_target_pairs={{6,0},{8,2},{10,4},{12,6},{14,8},{16,10},{18,12},{20,14},{22,16},{... | collective-permute-start | bytes 73736 | tf_op jit(solution)/shard_map/ppermute | solution.py:21
  284.4 40.7 %collective-permute-start.12 = (f32[8,3,256]{2,1,0:T(4,128)S(1)}, f32[8,3,256]{2,1,0:T(4,128)S(1)}, u32[]{:S(2)}, u32[]{:S(2)}) collective-permute-start(f32[8,3,256]{2,1,0:T(4,128)S(1)} %copy.288), channel_id=1, source_target_pairs={{8,0},{10,2},{12,4},{14,6},{16,8},{18,10},{20,12},{22,14},{24,16},... | collective-permute-start | bytes 73736 | tf_op jit(solution)/shard_map/ppermute | solution.py:21
  325.1 20.1 %copy-start.26 = (bf16[8,256,128]{2,1,0:T(8,128)(2,1)S(1)}, bf16[8,256,128]{2,1,0:T(8,128)(2,1)}, u32[]{:S(2)}) copy-start(bf16[8,256,128]{2,1,0:T(8,128)(2,1)} %get-tuple-element.9) | copy-start | bytes 1572868
  325.1 20.1 %copy-start.36 = (pred[8]{0:T(512)(128)(4,1)S(1)}, pred[8]{0:T(512)(128)(4,1)}, u32[]{:S(2)}) copy-start(pred[8]{0:T(512)(128)(4,1)} %get-tuple-element.141) | copy-start | bytes 28
  325.1 20.1 %copy-start.37 = (pred[8]{0:T(512)(128)(4,1)S(1)}, pred[8]{0:T(512)(128)(4,1)}, u32[]{:S(2)}) copy-start(pred[8]{0:T(512)(128)(4,1)} %get-tuple-element.139) | copy-start | bytes 28
  353.6 1.8 copy-start.1
  (7 other events, 4.8 us)
Sparse Core Ops, SparseCore 0:
  10.1 34.1 all-gather.3
  63.4 129.2 all-gather.5
  194.9 91.9 all-gather.7
